TPU v7x, 256 devices: a whole 4x4x8 slice. The times are simulated.
256 devices in a mesh: win: 32 (over x, y, core), exp: 8 (over z).
Axes of the slice: x: 4, y: 4, z: 8, core: 2. Of those that a mesh axis runs over, the one named last changes fastest.
Arguments:
- tokens: bfloat16 [16384, 2048], P('win'), may hold values from -9 to 9
- router: bfloat16 [2048, 32], replicated, may hold values from -0.125 to 0.125
- w_in: bfloat16 [32, 2048, 8192], P('win', None, 'exp'), may hold values from -0.125 to 0.125
- w_out: bfloat16 [32, 8192, 2048], P('win', 'exp'), may hold values from -0.0625 to 0.0625
- expert_ids: int32 [16384, 2], P('win'), may hold values from 0 to 31, all different within a row; in each aligned block of 512 rows (0 to 511, 512 to 1023, ...) at most 48 rows name the same one
- offsets: int32 [32], P('win'), may hold values from 0 to 63
Outputs:
- consensus_state: bfloat16 [16384, 2048], P('win', 'exp')
Inputs may be any that keep to these rules, and one draw needn't show every extreme that they name: `expert_ids`: in each window (an aligned block of 512 rows) no expert is named by more than 48 choices, a bound that some block reaches; a token's two experts differ.
All inputs are finite; a program needn't handle non-finite values.
Results may differ from a plain program's by a relative error of at most 0.015.
Values may be sent and summed in bfloat16 or wider, within the bound.
No kernel may reach another device: no remote copies, remote signals or barrier semaphores. Data moves between devices by JAX's collectives and lax.ppermute only.
A program may use at most 128 MiB of HBM per device.

v0:
```python
import math
import jax
import jax.numpy as jnp
from jax import lax
from jax.sharding import PartitionSpec as P

D = 2048
EXPERTS = 32
OV = 256
CAP = 48


def shifted(shard, axis, by):
    count = lax.axis_size(axis)
    pairs = [(i, i + by) for i in range(count) if 0 <= i + by < count]
    return lax.ppermute(shard, axis, pairs)


def shards(tokens, router, w_in, w_out, expert_ids, offsets):
    tok_count = tokens.shape[0]
    win_size = lax.axis_size("win")
    local_experts = w_in.shape[0]
    col_width = D // lax.axis_size("exp")
    flat_ids = expert_ids.reshape(-1)
    expert_order = jnp.arange(EXPERTS, dtype=jnp.int32)
    hit_table = (flat_ids[:, None] == expert_order[None, :]).astype(jnp.int32)
    rank_table = jnp.cumsum(hit_table, axis=0) - 1
    slot_index = jnp.sum(hit_table * rank_table, axis=1)
    slot_target = flat_ids * CAP + slot_index
    token_index = jnp.repeat(jnp.arange(tok_count, dtype=jnp.int32), 2)
    source_table = jnp.full((EXPERTS * CAP,), tok_count, jnp.int32).at[slot_target].set(token_index)
    padded = jnp.concatenate([tokens, jnp.zeros((1, D), tokens.dtype)], axis=0)
    outgoing = padded[source_table].reshape(win_size, local_experts, CAP, D)
    hidden_rows = jnp.einsum(
        "secd,edf->secf",
        lax.all_to_all(outgoing, "win", split_axis=0, concat_axis=0, tiled=True),
        w_in,
        preferred_element_type=jnp.float32,
    )
    hidden_rows = jax.nn.relu(hidden_rows).astype(jnp.bfloat16)
    results = jnp.einsum("secf,efd->secd", hidden_rows, w_out, preferred_element_type=jnp.float32)
    logits = jnp.dot(tokens, router, preferred_element_type=jnp.float32)
    first_hit = expert_ids[:, 0:1] == expert_order[None, :]
    second_hit = expert_ids[:, 1:2] == expert_order[None, :]
    logit_first = jnp.sum(jnp.where(first_hit, logits, 0.0), axis=1, keepdims=True)
    logit_second = jnp.sum(jnp.where(second_hit, logits, 0.0), axis=1, keepdims=True)
    gate_first = jax.nn.sigmoid(logit_first - logit_second)
    gate_second = jax.nn.sigmoid(logit_second - logit_first)
    returned = lax.all_to_all(results, "win", split_axis=0, concat_axis=0, tiled=True)
    flat_rows = returned.reshape(EXPERTS * CAP, returned.shape[-1])
    picked = flat_rows[slot_target].reshape(tok_count, 2, returned.shape[-1])
    expert_sum = lax.psum_scatter(
        gate_first * picked[:, 0] + gate_second * picked[:, 1],
        "exp",
        scatter_dimension=1,
        tiled=True,
    )
    own_cols = lax.dynamic_slice_in_dim(tokens, lax.axis_index("exp") * col_width, col_width, 1)
    layer_state = (own_cols.astype(jnp.float32) + expert_sum).astype(jnp.bfloat16)
    head_rows = layer_state[:OV]
    tail_rows = layer_state[tok_count - OV :]
    previous = shifted(tail_rows, "win", 1)
    contract = (((1,), (1,)), ((), ()))
    partial_scores = lax.dot_general(
        head_rows, previous, contract, preferred_element_type=jnp.float32
    )
    scores = lax.psum(partial_scores.astype(jnp.bfloat16), "exp").astype(jnp.float32)
    row_pos = jnp.arange(OV, dtype=jnp.int32)[:, None]
    col_pos = jnp.arange(OV, dtype=jnp.int32)[None, :]
    distance = jnp.abs(col_pos - row_pos - offsets[0]).astype(jnp.float32) * (8.0 / OV)
    scores = scores / math.sqrt(D) - distance
    weights = jax.nn.softmax(scores, axis=-1).astype(jnp.bfloat16)
    blended = jnp.dot(weights, previous, preferred_element_type=jnp.float32)
    mixed_rows = (0.5 * (head_rows.astype(jnp.float32) + blended)).astype(jnp.bfloat16)
    mixed_rows = jnp.where(lax.axis_index("win") > 0, mixed_rows, head_rows)
    return jnp.concatenate([mixed_rows, layer_state[OV:]], axis=0)


def solution(mesh):
    return jax.shard_map(
        shards,
        mesh=mesh,
        in_specs=(
            P("win", None),
            P(),
            P("win", None, "exp"),
            P("win", "exp", None),
            P("win", None),
            P("win"),
        ),
        out_specs=P("win", "exp"),
        check_vma=False,
    )
```

profile of v0, /device:TPU:2, one launch (start us, length us, event | category | flops | bytes accessed | tf_op | source)
XLA Modules:
  0.0 520.1 jit_solution(12146455405890550260)
XLA Ops:
  6.5 0.0 copy-start
  6.5 0.9 copy.15
  7.4 0.2 eq.67
  7.6 0.2 eq.63
  7.7 0.7 broadcast_multiply_fusion
  8.4 9.0 %reduce-window.6 = s32[32,8,128]{2,1,0:T(8,128)S(1)} reduce-window(s32[32,8,128]{2,1,0:T(8,128)S(1)} %fusion.20, s32[]{:T(128)} %constant.20.clone.1), window={size=1x1x128 pad=0_0x0_0x127_0}, to_apply=%region_2.3 | reduce-window | flops 4161536 | bytes 262148 | tf_op jit(solution)/shard_map/reduce-window
  17.5 0.1 slice.37
  17.6 0.1 copy.17
  17.7 0.1 copy.18
  17.8 0.1 add_add_fusion
  17.9 0.1 copy.14
  18.1 0.2 mul.54
  18.3 0.2 reshape.133
  18.5 4.3 scatter_custom_fusion
  22.9 1.7 concatenate.6
  24.6 7.1 %gather_fusion = bf16[1536,2048]{1,0:T(8,128)(2,1)} fusion(bf16[513,2048]{1,0:T(8,128)(2,1)S(1)} %concatenate.6, s32[2048]{0:T(1024)S(1)} %pad_clamp_fusion), kind=kCustom, calls=%fused_computation | custom fusion | bytes 12589056 | tf_op jit(solution)/shard_map/gather | solution.py:33
  31.7 0.0 copy-start.3
  31.7 78.5 %all_to_all.10 = bf16[32,1,48,2048]{3,2,1,0:T(8,128)(2,1)S(1)} all-to-all(bf16[32,1,48,2048]{3,2,1,0:T(8,128)(2,1)} %bitcast.61), channel_id=1, replica_groups=mesh['win'=32,'exp'=8] {'win'}, dimensions={0} | all-to-all | bytes 12582912 | tf_op jit(solution)/shard_map/all_to_all | solution.py:36
  110.2 0.0 copy-done.3
  110.2 0.0 copy-start.4
  110.2 6.8 %fusion = bf16[32,48,1024]{2,1,0:T(8,128)(2,1)S(1)} fusion(bf16[32,1,48,2048]{3,2,1,0:T(8,128)(2,1)S(1)} %all_to_all.10, bf16[1,2048,1024]{2,1,0:T(8,128)(2,1)S(1)} %copy-done.3), kind=kOutput, calls=%fused_computation.3 | convolution fusion | flops 6442450944 | bytes 13631488 | tf_op jit(solution)/shard_map/secd,edf->secf/dot_general | solution.py:34
  117.0 0.0 copy-done.4
  117.0 9.1 %convolution_bitcast_fusion = f32[32,1,48,2048]{3,2,1,0:T(8,128)} fusion(bf16[1,1024,2048]{2,1,0:T(8,128)(2,1)S(1)} %copy-done.4, bf16[32,48,1024]{2,1,0:T(8,128)(2,1)S(1)} %fusion), kind=kOutput, calls=%fused_computation.6 | convolution fusion | flops 6447169536 | bytes 19922944 | tf_op jit(solution)/shard_map/secf,efd->secd/dot_general | solution.py:41
  126.1 0.0 copy-start.2
  126.1 7.4 %all-to-all-start.1 = ((f32[32,1,48,2048]{3,2,1,0:T(8,128)}), f32[32,1,48,2048]{3,2,1,0:T(8,128)}, u32[]{:S(2)}, u32[]{:S(2)}) async-start(f32[32,1,48,2048]{3,2,1,0:T(8,128)} %convolution_bitcast_fusion), calls=%async_computation.1 | async-start | bytes 25165824 | tf_op jit(solution)/shard_map/all_to_all | solution.py:49
  133.5 0.2 reduce-scatter.2.cloned.1.call-start
  133.8 0.0 copy-done.2
  133.8 0.0 copy-done
  133.8 0.0 copy-done.1
  133.8 0.8 select_reduce_fusion.1
  134.6 165.8 %all-to-all-done.1 = f32[32,1,48,2048]{3,2,1,0:T(8,128)} async-done(((f32[32,1,48,2048]{3,2,1,0:T(8,128)}), f32[32,1,48,2048]{3,2,1,0:T(8,128)}, u32[]{:S(2)}, u32[]{:S(2)}) %all-to-all-start.1) | async-done | bytes 12582944 | tf_op jit(solution)/shard_map/all_to_all | solution.py:49
  300.4 13.6 %gather_fusion.1 = f32[1024,2048]{1,0:T(8,128)} fusion(f32[1536,2048]{1,0:T(8,128)} %bitcast.17, s32[1024]{0:T(1024)S(1)} %broadcast_clamp_fusion), kind=kCustom, calls=%fused_computation.1 | custom fusion | bytes 16781312 | tf_op jit(solution)/shard_map/gather | solution.py:51
  314.1 10.6 %reshape.112 = f32[512,2,2048]{2,1,0:T(2,128)} reshape(f32[1024,2048]{1,0:T(8,128)} %gather_fusion.1) | data formatting | bytes 16777216 | tf_op jit(solution)/shard_map/reshape | solution.py:51
  324.6 11.0 %fusion.27 = (f32[512,1,2048]{2,1,0:T(1,128)S(1)}, f32[512,1,2048]{2,1,0:T(1,128)S(1)}) fusion(f32[512,2,2048]{2,1,0:T(2,128)} %reshape.112), kind=kLoop, calls=%fused_computation.56 | loop fusion | bytes 16777216 | tf_op jit(solution)/shard_map/slice | solution.py:53
  335.7 6.7 %fusion.3 = f32[512,2048]{1,0:T(8,128)} fusion(f32[512,1,2048]{2,1,0:T(1,128)S(1)} %get-tuple-element.8, f32[512,1,2048]{2,1,0:T(1,128)S(1)} %get-tuple-element.7, f32[512]{0:T(512)S(1)} %get-tuple-element.10, f32[512]{0:T(512)S(1)} %get-tuple-element.9), kind=kLoop, calls=%fused_computation.9 | loop fusion | flops 3145728 | bytes 12587008 | tf_op jit(solution)/shard_map/add | solution.py:53
  342.4 0.0 reduce-scatter.2.cloned.1.call-update
  342.4 0.0 all-reduce.3.cloned.1.call-start
  342.5 87.0 %reduce-scatter.2.cloned.1.call-done = f32[512,256]{1,0:T(8,128)} async-done(((f32[512,2048]{1,0:T(8,128)}), f32[512,256]{1,0:T(8,128)}) %reduce-scatter.2.cloned.1.call-update) | async-done | bytes 524304 | tf_op jit(solution)/shard_map/reduce_scatter | solution.py:52
  429.5 1.1 add_convert_fusion
  430.7 1.9 collective-permute-start
  432.6 6.5 %collective-permute-done = bf16[256,256]{1,0:T(8,128)(2,1)S(1)} collective-permute-done((bf16[256,256]{1,0:T(8,128)(2,1)S(1)}, bf16[256,256]{1,0:T(8,128)(2,1)S(1)}, u32[]{:S(2)}, u32[]{:S(2)}) %collective-permute-start) | collective-permute-done | bytes 131104 | tf_op jit(solution)/shard_map/ppermute | solution.py:16
  439.1 0.9 convolution_convert_fusion
  439.9 0.0 all-reduce.3.cloned.1.call-update
  440.6 68.6 %all-reduce.3.cloned.1.call-done = bf16[256,256]{1,0:T(8,128)(2,1)} async-done(((bf16[256,256]{1,0:T(8,128)(2,1)}), bf16[256,256]{1,0:T(8,128)(2,1)}) %all-reduce.3.cloned.1.call-update) | async-done | bytes 131088 | tf_op jit(solution)/shard_map/psum | solution.py:67
  509.2 1.1 fusion.11
  510.3 1.1 fusion.12
  511.4 1.2 fusion.10
  512.6 0.7 pad_maximum_fusion
  (13 shorter events, 0.2 us)
Async XLA Ops:
  6.5 127.3 %copy-start = (bf16[2048,32]{0,1:T(8,128)(2,1)S(1)}, bf16[2048,32]{0,1:T(8,128)(2,1)}, u32[]{:S(2)}) copy-start(bf16[2048,32]{0,1:T(8,128)(2,1)} %param.7) | copy-start | bytes 393220
  31.7 78.5 %copy-start.3 = (bf16[1,2048,1024]{2,1,0:T(8,128)(2,1)S(1)}, bf16[1,2048,1024]{2,1,0:T(8,128)(2,1)}, u32[]{:S(2)}) copy-start(bf16[1,2048,1024]{2,1,0:T(8,128)(2,1)} %param.8) | copy-start | bytes 12582916
  110.2 6.8 %copy-start.4 = (bf16[1,1024,2048]{2,1,0:T(8,128)(2,1)S(1)}, bf16[1,1024,2048]{2,1,0:T(8,128)(2,1)}, u32[]{:S(2)}) copy-start(bf16[1,1024,2048]{2,1,0:T(8,128)(2,1)} %param.9) | copy-start | bytes 12582916
  126.1 7.7 %copy-start.2 = (s32[512,2]{0,1:T(2,128)S(1)}, s32[512,2]{0,1:T(2,128)}, u32[]{:S(2)}) copy-start(s32[512,2]{0,1:T(2,128)} %param.10) | copy-start | bytes 12292
  126.1 7.7 %copy-start.1 = (bf16[512,2048]{1,0:T(8,128)(2,1)S(1)}, bf16[512,2048]{1,0:T(8,128)(2,1)}, u32[]{:S(2)}) copy-start(bf16[512,2048]{1,0:T(8,128)(2,1)} %param.6) | copy-start | bytes 6291460
  126.1 174.3 %all-to-all-start.1 = ((f32[32,1,48,2048]{3,2,1,0:T(8,128)}), f32[32,1,48,2048]{3,2,1,0:T(8,128)}, u32[]{:S(2)}, u32[]{:S(2)}) async-start(f32[32,1,48,2048]{3,2,1,0:T(8,128)} %convolution_bitcast_fusion), calls=%async_computation.1 | async-start | bytes 25165824 | tf_op jit(solution)/shard_map/all_to_all | solution.py:49
  133.5 296.0 %reduce-scatter.2.cloned.1.call-start = ((), (), s32[]{:S(2)}) async-start(), calls=%async_computation.3 | async-start | bytes 4718592 | tf_op jit(solution)/shard_map/reduce_scatter | solution.py:52
  342.4 166.8 %all-reduce.3.cloned.1.call-start = ((), (), s32[]{:S(2)}) async-start(), calls=%async_computation.4 | async-start | bytes 262144 | tf_op jit(solution)/shard_map/psum | solution.py:67
  430.7 8.4 %collective-permute-start = (bf16[256,256]{1,0:T(8,128)(2,1)S(1)}, bf16[256,256]{1,0:T(8,128)(2,1)S(1)}, u32[]{:S(2)}, u32[]{:S(2)}) collective-permute-start(bf16[256,256]{1,0:T(8,128)(2,1)S(1)} %slice.42), channel_id=1, source_target_pairs={{0,8},{8,16},{16,24},{24,32},{32,40},{40,48},{48,56},{56,64},{64,7... | collective-permute-start | bytes 393224 | tf_op jit(solution)/shard_map/ppermute | solution.py:16
Sparse Core Ops, SparseCore 0:
  342.5 86.9 reduce-scatter.1
  440.1 69.0 all-reduce.2
where the time goes:
time: 521 us; the launch traced here: 520 us
  waiting for transfers between devices  328 us (63%)
  blocking collectives  78.5 us (15%)
  local copies, waits for them, and re-layouts  50.4 us (10%)
  other arithmetic  20.7 us (4%)
  matrix products  18.7 us (4%)
  between operations  14.3 us (3%)
  starting transfers between devices  9.6 us (2%)
    all_to_all x1, waiting for transfers between devices, shards(): lax.all_to_all(results, 'win', split_axis=0, concat_axis=0, tiled=True)  166 us
    reduce_scatter x1, waiting for transfers between devices, shards(): lax.psum_scatter(gate_first * picked[:, 0] + gate_second * picked[:, 1],...  87 us
    all_to_all x1, blocking collectives, shards(): lax.all_to_all(outgoing, 'win', split_axis=0, concat_axis=0, tiled=True)  78.5 us
    psum x1, waiting for transfers between devices, shards(): lax.psum(partial_scores.astype(jnp.bfloat16), 'exp').astype(jnp.float32)  68.6 us
    gather x1, local copies, waits for them, and re-layouts, shards(): picked = flat_rows[slot_target].reshape(tok_count, 2, returned.shape[-1])  13.6 us
    slice x1, local copies, waits for them, and re-layouts, shards(): picked[:, 0]  11 us
    reshape x1, local copies, waits for them, and re-layouts, shards(): picked = flat_rows[slot_target].reshape(tok_count, 2, returned.shape[-1])  10.6 us
  transfers between devices with their start and end apart: 4, of which 4 were waited for; matrix products, arithmetic and copies ran while one was open for 0% of the time, Pallas kernels for 0%

commit v1 on v0

--- a/solution.py
+++ b/solution.py
@@ -1,3 +1,4 @@
+import functools
 import math
 import jax
 import jax.numpy as jnp
@@ -8,6 +9,15 @@
 EXPERTS = 32
 OV = 256
 CAP = 48
+
+
+def number_targets(load, mesh_name):
+    vec_out = jax.lax.all_gather(load, mesh_name)
+    fresh = jnp.sum(vec_out, axis=0)
+    return fresh
+
+
+refer_the_tiles = functools.partial(number_targets, mesh_name="exp")
 
 
 def shifted(shard, axis, by):
@@ -64,7 +74,7 @@
     partial_scores = lax.dot_general(
         head_rows, previous, contract, preferred_element_type=jnp.float32
     )
-    scores = lax.psum(partial_scores.astype(jnp.bfloat16), "exp").astype(jnp.float32)
+    scores = refer_the_tiles(partial_scores.astype(jnp.bfloat16)).astype(jnp.float32)
     row_pos = jnp.arange(OV, dtype=jnp.int32)[:, None]
     col_pos = jnp.arange(OV, dtype=jnp.int32)[None, :]
     distance = jnp.abs(col_pos - row_pos - offsets[0]).astype(jnp.float32) * (8.0 / OV)

time: 521 us -> 485 us (0.931)
  waiting for transfers between devices: 328 us -> 294 us
    psum x1 -> x0, waiting for transfers between devices: 68.6 us -> none  [shards(): lax.psum(partial_scores.astype(jnp.bfloat16), 'exp').astype(jnp.float32)]
    all_gather x0 -> x1, waiting for transfers between devices: none -> 34.4 us  [number_targets(): vec_out = jax.lax.all_gather(load, mesh_name)]
where the time goes in v1:
time: 485 us
  waiting for transfers between devices  294 us (61%)
  blocking collectives  78.5 us (16%)
  local copies, waits for them, and re-layouts  50.4 us (10%)
  other arithmetic  20.3 us (4%)
  matrix products  17.8 us (4%)
  between operations  14.3 us (3%)
  starting transfers between devices  9.6 us (2%)
    all_to_all x1, waiting for transfers between devices, shards(): lax.all_to_all(results, 'win', split_axis=0, concat_axis=0, tiled=True)  166 us
    reduce_scatter x1, waiting for transfers between devices, shards(): lax.psum_scatter(gate_first * picked[:, 0] + gate_second * picked[:, 1],...  87 us
    all_to_all x1, blocking collectives, shards(): lax.all_to_all(outgoing, 'win', split_axis=0, concat_axis=0, tiled=True)  78.5 us
    all_gather x1, waiting for transfers between devices, number_targets(): vec_out = jax.lax.all_gather(load, mesh_name)  34.4 us
    gather x1, local copies, waits for them, and re-layouts, shards(): picked = flat_rows[slot_target].reshape(tok_count, 2, returned.shape[-1])  13.6 us
    slice x1, local copies, waits for them, and re-layouts, shards(): picked[:, 0]  11 us
    reshape x1, local copies, waits for them, and re-layouts, shards(): picked = flat_rows[slot_target].reshape(tok_count, 2, returned.shape[-1])  10.6 us
  transfers between devices with their start and end apart: 4, of which 4 were waited for; matrix products, arithmetic and copies ran while one was open for 0% of the time, Pallas kernels for 0%

profile of v1, /device:TPU:2, one launch (start us, length us, event | category | flops | bytes accessed | tf_op | source)
XLA Modules:
  0.0 484.7 jit_solution(4257872956064617419)
XLA Ops:
  6.5 0.0 copy-start
  6.5 0.9 copy.24
  7.4 0.2 eq.67
  7.6 0.2 eq.63
  7.7 0.7 broadcast_multiply_fusion
  8.4 9.0 %reduce-window.6 = s32[32,8,128]{2,1,0:T(8,128)S(1)} reduce-window(s32[32,8,128]{2,1,0:T(8,128)S(1)} %fusion.20, s32[]{:T(128)} %constant.20.clone.1), window={size=1x1x128 pad=0_0x0_0x127_0}, to_apply=%region_2.3 | reduce-window | flops 4161536 | bytes 262148 | tf_op jit(solution)/shard_map/reduce-window
  17.5 0.1 slice.37
  17.6 0.1 copy.26
  17.7 0.1 copy.27
  17.8 0.1 add_add_fusion
  17.9 0.1 copy.23
  18.1 0.2 mul.54
  18.3 0.2 reshape.133
  18.5 4.3 scatter_custom_fusion
  22.9 1.7 concatenate.6
  24.6 7.1 %gather_fusion = bf16[1536,2048]{1,0:T(8,128)(2,1)} fusion(bf16[513,2048]{1,0:T(8,128)(2,1)S(1)} %concatenate.6, s32[2048]{0:T(1024)S(1)} %pad_clamp_fusion), kind=kCustom, calls=%fused_computation | custom fusion | bytes 12589056 | tf_op jit(solution)/shard_map/gather | solution.py:43
  31.7 0.0 copy-start.3
  31.7 78.5 %all_to_all.10 = bf16[32,1,48,2048]{3,2,1,0:T(8,128)(2,1)S(1)} all-to-all(bf16[32,1,48,2048]{3,2,1,0:T(8,128)(2,1)} %bitcast.62), channel_id=1, replica_groups=mesh['win'=32,'exp'=8] {'win'}, dimensions={0} | all-to-all | bytes 12582912 | tf_op jit(solution)/shard_map/all_to_all | solution.py:46
  110.2 0.0 copy-done.3
  110.2 0.0 copy-start.4
  110.2 6.8 %fusion = bf16[32,48,1024]{2,1,0:T(8,128)(2,1)S(1)} fusion(bf16[32,1,48,2048]{3,2,1,0:T(8,128)(2,1)S(1)} %all_to_all.10, bf16[1,2048,1024]{2,1,0:T(8,128)(2,1)S(1)} %copy-done.3), kind=kOutput, calls=%fused_computation.3 | convolution fusion | flops 6442450944 | bytes 13631488 | tf_op jit(solution)/shard_map/secd,edf->secf/dot_general | solution.py:44
  117.0 0.0 copy-done.4
  117.0 9.1 %convolution_bitcast_fusion = f32[32,1,48,2048]{3,2,1,0:T(8,128)} fusion(bf16[1,1024,2048]{2,1,0:T(8,128)(2,1)S(1)} %copy-done.4, bf16[32,48,1024]{2,1,0:T(8,128)(2,1)S(1)} %fusion), kind=kOutput, calls=%fused_computation.6 | convolution fusion | flops 6447169536 | bytes 19922944 | tf_op jit(solution)/shard_map/secf,efd->secd/dot_general | solution.py:51
  126.1 7.4 %all-to-all-start.1 = ((f32[32,1,48,2048]{3,2,1,0:T(8,128)}), f32[32,1,48,2048]{3,2,1,0:T(8,128)}, u32[]{:S(2)}, u32[]{:S(2)}) async-start(f32[32,1,48,2048]{3,2,1,0:T(8,128)} %convolution_bitcast_fusion), calls=%async_computation.1 | async-start | bytes 25165824 | tf_op jit(solution)/shard_map/all_to_all | solution.py:59
  133.5 0.2 reduce-scatter.2.cloned.1.call-start
  133.8 0.0 copy-done.2
  133.8 0.0 copy-done
  133.8 0.0 copy-done.1
  133.8 0.8 select_reduce_fusion.1
  134.6 165.8 %all-to-all-done.1 = f32[32,1,48,2048]{3,2,1,0:T(8,128)} async-done(((f32[32,1,48,2048]{3,2,1,0:T(8,128)}), f32[32,1,48,2048]{3,2,1,0:T(8,128)}, u32[]{:S(2)}, u32[]{:S(2)}) %all-to-all-start.1) | async-done | bytes 12582944 | tf_op jit(solution)/shard_map/all_to_all | solution.py:59
  300.4 13.6 %gather_fusion.1 = f32[1024,2048]{1,0:T(8,128)} fusion(f32[1536,2048]{1,0:T(8,128)} %bitcast.17, s32[1024]{0:T(1024)S(1)} %broadcast_clamp_fusion), kind=kCustom, calls=%fused_computation.1 | custom fusion | bytes 16781312 | tf_op jit(solution)/shard_map/gather | solution.py:61
  314.1 10.6 %reshape.112 = f32[512,2,2048]{2,1,0:T(2,128)} reshape(f32[1024,2048]{1,0:T(8,128)} %gather_fusion.1) | data formatting | bytes 16777216 | tf_op jit(solution)/shard_map/reshape | solution.py:61
  324.6 11.0 %fusion.27 = (f32[512,1,2048]{2,1,0:T(1,128)S(1)}, f32[512,1,2048]{2,1,0:T(1,128)S(1)}) fusion(f32[512,2,2048]{2,1,0:T(2,128)} %reshape.112), kind=kLoop, calls=%fused_computation.56 | loop fusion | bytes 16777216 | tf_op jit(solution)/shard_map/slice | solution.py:63
  335.7 6.7 %fusion.3 = f32[512,2048]{1,0:T(8,128)} fusion(f32[512,1,2048]{2,1,0:T(1,128)S(1)} %get-tuple-element.8, f32[512,1,2048]{2,1,0:T(1,128)S(1)} %get-tuple-element.7, f32[512]{0:T(512)S(1)} %get-tuple-element.10, f32[512]{0:T(512)S(1)} %get-tuple-element.9), kind=kLoop, calls=%fused_computation.9 | loop fusion | flops 3145728 | bytes 12587008 | tf_op jit(solution)/shard_map/add | solution.py:63
  342.4 0.0 reduce-scatter.2.cloned.1.call-update
  342.4 0.0 all-gather.3.cloned.1.call-start
  342.5 87.0 %reduce-scatter.2.cloned.1.call-done = f32[512,256]{1,0:T(8,128)} async-done(((f32[512,2048]{1,0:T(8,128)}), f32[512,256]{1,0:T(8,128)}) %reduce-scatter.2.cloned.1.call-update) | async-done | bytes 524304 | tf_op jit(solution)/shard_map/reduce_scatter | solution.py:62
  429.5 1.1 add_convert_fusion
  430.7 1.9 collective-permute-start
  432.6 6.5 %collective-permute-done = bf16[256,256]{1,0:T(8,128)(2,1)S(1)} collective-permute-done((bf16[256,256]{1,0:T(8,128)(2,1)S(1)}, bf16[256,256]{1,0:T(8,128)(2,1)S(1)}, u32[]{:S(2)}, u32[]{:S(2)}) %collective-permute-start) | collective-permute-done | bytes 131104 | tf_op jit(solution)/shard_map/ppermute | solution.py:26
  439.1 0.9 convolution_convert_fusion
  439.9 0.0 all-gather.3.cloned.1.call-update
  440.6 34.4 %all-gather.3.cloned.1.call-done = bf16[2048,256]{1,0:T(8,128)(2,1)} async-done(((bf16[256,256]{1,0:T(8,128)(2,1)}), bf16[2048,256]{1,0:T(8,128)(2,1)}) %all-gather.3.cloned.1.call-update) | async-done | bytes 1048592 | tf_op jit(solution)/shard_map/all_gather | solution.py:15
  475.1 1.4 reduce_sum.54
  476.4 0.2 fusion.11
  476.6 0.2 fusion.12
  476.8 0.3 fusion.10
  477.1 0.7 pad_maximum_fusion
  (14 shorter events, 0.2 us)
Async XLA Ops:
  6.5 127.3 %copy-start = (bf16[2048,32]{0,1:T(8,128)(2,1)S(1)}, bf16[2048,32]{0,1:T(8,128)(2,1)}, u32[]{:S(2)}) copy-start(bf16[2048,32]{0,1:T(8,128)(2,1)} %param.7) | copy-start | bytes 393220
  31.7 78.5 %copy-start.3 = (bf16[1,2048,1024]{2,1,0:T(8,128)(2,1)S(1)}, bf16[1,2048,1024]{2,1,0:T(8,128)(2,1)}, u32[]{:S(2)}) copy-start(bf16[1,2048,1024]{2,1,0:T(8,128)(2,1)} %param.8) | copy-start | bytes 12582916
  110.2 6.8 %copy-start.4 = (bf16[1,1024,2048]{2,1,0:T(8,128)(2,1)S(1)}, bf16[1,1024,2048]{2,1,0:T(8,128)(2,1)}, u32[]{:S(2)}) copy-start(bf16[1,1024,2048]{2,1,0:T(8,128)(2,1)} %param.9) | copy-start | bytes 12582916
  126.1 7.7 %copy-start.2 = (s32[512,2]{0,1:T(2,128)S(1)}, s32[512,2]{0,1:T(2,128)}, u32[]{:S(2)}) copy-start(s32[512,2]{0,1:T(2,128)} %param.10) | copy-start | bytes 12292
  126.1 7.7 %copy-start.1 = (bf16[512,2048]{1,0:T(8,128)(2,1)S(1)}, bf16[512,2048]{1,0:T(8,128)(2,1)}, u32[]{:S(2)}) copy-start(bf16[512,2048]{1,0:T(8,128)(2,1)} %param.6) | copy-start | bytes 6291460
  126.1 174.3 %all-to-all-start.1 = ((f32[32,1,48,2048]{3,2,1,0:T(8,128)}), f32[32,1,48,2048]{3,2,1,0:T(8,128)}, u32[]{:S(2)}, u32[]{:S(2)}) async-start(f32[32,1,48,2048]{3,2,1,0:T(8,128)} %convolution_bitcast_fusion), calls=%async_computation.1 | async-start | bytes 25165824 | tf_op jit(solution)/shard_map/all_to_all | solution.py:59
  133.5 296.0 %reduce-scatter.2.cloned.1.call-start = ((), (), s32[]{:S(2)}) async-start(), calls=%async_computation.3 | async-start | bytes 4718592 | tf_op jit(solution)/shard_map/reduce_scatter | solution.py:62
  342.4 132.6 %all-gather.3.cloned.1.call-start = ((), (), s32[]{:S(2)}) async-start(), calls=%async_computation.4 | async-start | bytes 1179648 | tf_op jit(solution)/shard_map/all_gather | solution.py:15
  430.7 8.4 %collective-permute-start = (bf16[256,256]{1,0:T(8,128)(2,1)S(1)}, bf16[256,256]{1,0:T(8,128)(2,1)S(1)}, u32[]{:S(2)}, u32[]{:S(2)}) collective-permute-start(bf16[256,256]{1,0:T(8,128)(2,1)S(1)} %slice.42), channel_id=1, source_target_pairs={{0,8},{8,16},{16,24},{24,32},{32,40},{40,48},{48,56},{56,64},{64,7... | collective-permute-start | bytes 393224 | tf_op jit(solution)/shard_map/ppermute | solution.py:26
Sparse Core Ops, SparseCore 0:
  342.5 86.9 reduce-scatter.1
  440.1 34.9 all-gather.2
